TPU v7x, 512 devices: a whole 4x4x16 slice. The times are simulated.
512 devices in a mesh: box: 8 (over z_lo, core), panel: 64 (over y, x, z_hi).
Axes of the slice: x: 4, y: 4, z: 16 (z_hi: 4, z_lo: 4; z = z_hi * 4 + z_lo), core: 2. Of those that a mesh axis runs over, the one named last changes fastest.
Arguments:
- exterior_rows: float32 [8, 2048, 2, 128], P('box'), may hold values from -6 to 6
- exterior_block: float32 [8, 6144, 2, 128], P('box', 'panel'), may hold values from -6 to 6
- shared_block: float32 [8, 2048, 2, 2048], P('box', 'panel'), may hold values from -0.9 to 0.9
- crossing_block: float32 [8, 6144, 2, 2048], P('box', 'panel'), may hold values from -0.125 to 0.125
Outputs:
- merged_map: float32 [8, 2, 6144, 2, 128], P('box', None, 'panel')
All inputs are finite; a program needn't handle non-finite values.
Results may differ from a plain program's by a relative error of at most 0.0001.
Values sent between devices are 32-bit elements; how exact they have to be, the bound alone decides.
No kernel may reach another device: no remote copies, remote signals or barrier semaphores. Data moves between devices by JAX's collectives and lax.ppermute only.
A program may use at most 64 MiB of HBM per device.

v0:
```python
import jax
import jax.numpy as jnp
from jax import lax
from jax.sharding import PartitionSpec as P

ITERS = 3


def swapped(shard, axis, bit):
    return lax.ppermute(shard, axis, [(i, i ^ 1 << bit) for i in range(lax.axis_size(axis))])


def complex_product(left_factor, operand):
    highest = lax.Precision.HIGHEST
    real_part = jnp.dot(
        left_factor[:, 0], operand[:, 0], precision=highest, preferred_element_type=jnp.float32
    ) - jnp.dot(
        left_factor[:, 1], operand[:, 1], precision=highest, preferred_element_type=jnp.float32
    )
    imag_part = jnp.dot(
        left_factor[:, 0], operand[:, 1], precision=highest, preferred_element_type=jnp.float32
    ) + jnp.dot(
        left_factor[:, 1], operand[:, 0], precision=highest, preferred_element_type=jnp.float32
    )
    return jnp.stack([real_part, imag_part], axis=1)


def slice_product(matrix, gathered_piece):
    return complex_product(matrix, gathered_piece)


def local(exterior_rows, exterior_block, shared_block, crossing_block):
    start_rows = exterior_rows[0]
    own_exterior = exterior_block[0]
    own_shared = shared_block[0]
    own_crossing = crossing_block[0]
    width_panel = own_shared.shape[0]
    panel_index = lax.axis_index("panel")
    own_rows = lax.dynamic_slice_in_dim(start_rows, panel_index * width_panel, width_panel, 0)
    other_form, other_crossing = swapped((own_shared, own_crossing), "box", 0)

    def through_own(gathered_piece):
        return slice_product(own_shared, gathered_piece)

    def own_step(image_now):
        return own_rows + through_own(lax.all_gather(image_now, "panel", axis=0, tiled=True))

    image_panel = complex_product(other_form, start_rows)
    rows_panel = own_step(image_panel)
    for iteration in range(1, ITERS):
        image_panel = slice_product(
            other_form, lax.all_gather(rows_panel, "panel", axis=0, tiled=True)
        )
        rows_panel = own_step(image_panel)
    gathered_piece = lax.all_gather(rows_panel, "panel", axis=0, tiled=True)
    image_final = slice_product(other_form, gathered_piece)
    other_terms = slice_product(other_crossing, gathered_piece)
    own_terms = slice_product(
        own_crossing, lax.all_gather(image_final, "panel", axis=0, tiled=True)
    )
    merged = jnp.stack([own_exterior + own_terms, -other_terms], axis=0)
    return merged[None]


def solution(mesh):
    return jax.shard_map(
        local,
        mesh=mesh,
        in_specs=(
            P("box", None, None, None),
            P("box", "panel", None, None),
            P("box", "panel", None, None),
            P("box", "panel", None, None),
        ),
        out_specs=P("box", None, "panel", None, None),
        check_vma=False,
    )
```

profile of v0, /device:TPU:4, one launch (start us, length us, event | category | flops | bytes accessed | tf_op | source)
XLA Modules:
  0.0 853.4 jit_solution(4631152785487353609)
XLA Ops:
  6.5 1.9 collective-permute-start
  8.5 4.0 fusion.108
  17.6 119.2 %all-gather.8.cloned.1.call-done = f32[2048,2,128]{2,0,1:T(8,128)} async-done(((f32[32,2,128]{2,0,1:T(8,128)}), f32[2048,2,128]{2,0,1:T(8,128)}) %all-gather.8.cloned.1.call-update) | async-done | bytes 2097168 | tf_op jit(solution)/shard_map/all_gather | solution.py:46
  136.8 2.1 fusion.19
  138.9 2.0 fusion.18
  143.1 110.5 %all-gather.10.cloned.1.call-done = f32[2048,2,128]{2,0,1:T(8,128)} async-done(((f32[32,2,128]{2,0,1:T(8,128)}), f32[2048,2,128]{2,0,1:T(8,128)}) %all-gather.10.cloned.1.call-update) | async-done | bytes 2097168 | tf_op jit(solution)/shard_map/all_gather | solution.py:52
  253.6 2.1 fusion.20
  255.8 2.0 fusion.21
  260.1 110.3 %all-gather.12.cloned.1.call-done = f32[2048,2,128]{2,0,1:T(8,128)} async-done(((f32[32,2,128]{2,0,1:T(8,128)}), f32[2048,2,128]{2,0,1:T(8,128)}) %all-gather.12.cloned.1.call-update) | async-done | bytes 2097168 | tf_op jit(solution)/shard_map/all_gather | solution.py:46
  370.5 2.1 fusion.23
  372.6 2.0 fusion.22
  376.8 110.5 %all-gather.14.cloned.1.call-done = f32[2048,2,128]{2,0,1:T(8,128)} async-done(((f32[32,2,128]{2,0,1:T(8,128)}), f32[2048,2,128]{2,0,1:T(8,128)}) %all-gather.14.cloned.1.call-update) | async-done | bytes 2097168 | tf_op jit(solution)/shard_map/all_gather | solution.py:52
  487.3 2.1 fusion.24
  489.5 2.0 fusion.25
  493.7 110.5 %all-gather.16.cloned.1.call-done = f32[2048,2,128]{2,0,1:T(8,128)} async-done(((f32[32,2,128]{2,0,1:T(8,128)}), f32[2048,2,128]{2,0,1:T(8,128)}) %all-gather.16.cloned.1.call-update) | async-done | bytes 2097168 | tf_op jit(solution)/shard_map/all_gather | solution.py:46
  604.2 2.1 fusion.27
  606.3 2.0 fusion.26
  610.5 110.5 %all-gather.18.cloned.1.call-done = f32[2048,2,128]{2,0,1:T(8,128)} async-done(((f32[32,2,128]{2,0,1:T(8,128)}), f32[2048,2,128]{2,0,1:T(8,128)}) %all-gather.18.cloned.1.call-update) | async-done | bytes 2097168 | tf_op jit(solution)/shard_map/all_gather | solution.py:55
  721.0 2.1 fusion.31
  723.2 2.0 fusion.33
  727.3 2.1 collective-permute-start.1
  729.4 4.5 fusion.109
  733.9 1.2 fusion.110
  735.1 1.3 fusion.30
  736.4 1.3 fusion
  737.7 1.3 fusion.32
  738.9 1.3 fusion.1
  740.2 97.6 %all-gather.20.cloned.1.call-done = f32[2048,2,128]{2,0,1:T(8,128)} async-done(((f32[32,2,128]{2,0,1:T(8,128)}), f32[2048,2,128]{2,0,1:T(8,128)}) %all-gather.20.cloned.1.call-update) | async-done | bytes 2097168 | tf_op jit(solution)/shard_map/all_gather | solution.py:59
  837.9 2.6 fusion.29
  840.4 2.4 fusion.28
  842.9 1.2 fusion.2
  844.1 1.2 fusion.3
  (66 shorter events, 19.4 us)
Async XLA Ops:
  6.5 130.3 %all-gather.8.cloned.1.call-start = ((), (), s32[]{:S(2)}) async-start(), calls=%async_computation | async-start | bytes 2129920 | tf_op jit(solution)/shard_map/all_gather | solution.py:46
  6.5 6.0 collective-permute-start
  13.6 3.6 copy-start.8
  16.4 237.2 %all-gather.10.cloned.1.call-start = ((), (), s32[]{:S(2)}) async-start(), calls=%async_computation.1 | async-start | bytes 2129920 | tf_op jit(solution)/shard_map/all_gather | solution.py:52
  136.8 4.1 copy-start.2
  143.1 227.4 %all-gather.12.cloned.1.call-start = ((), (), s32[]{:S(2)}) async-start(), calls=%async_computation.2 | async-start | bytes 2129920 | tf_op jit(solution)/shard_map/all_gather | solution.py:46
  253.6 4.1 copy-start.4
  259.9 227.4 %all-gather.14.cloned.1.call-start = ((), (), s32[]{:S(2)}) async-start(), calls=%async_computation.3 | async-start | bytes 2129920 | tf_op jit(solution)/shard_map/all_gather | solution.py:52
  370.5 4.1 copy-start.5
  376.8 227.4 %all-gather.16.cloned.1.call-start = ((), (), s32[]{:S(2)}) async-start(), calls=%async_computation.4 | async-start | bytes 2129920 | tf_op jit(solution)/shard_map/all_gather | solution.py:46
  487.3 4.1 copy-start.6
  493.6 227.4 %all-gather.18.cloned.1.call-start = ((), (), s32[]{:S(2)}) async-start(), calls=%async_computation.5 | async-start | bytes 2129920 | tf_op jit(solution)/shard_map/all_gather | solution.py:55
  604.2 4.1 copy-start.3
  610.5 227.4 %all-gather.20.cloned.1.call-start = ((), (), s32[]{:S(2)}) async-start(), calls=%async_computation.6 | async-start | bytes 2129920 | tf_op jit(solution)/shard_map/all_gather | solution.py:59
  721.0 4.1 copy-start
  727.3 6.6 collective-permute-start.1
  740.2 102.7 %copy-start.7 = (f32[96,1,2048]{2,1,0:T(1,128)S(1)}, f32[96,1,2048]{2,1,0:T(1,128)}, u32[]{:S(2)}) copy-start(f32[96,1,2048]{2,1,0:T(1,128)} %get-tuple-element.7) | copy-start | bytes 2359300
  837.9 5.0 copy-start.1
  842.8 2.4 copy-start.9
Sparse Core Ops, SparseCore 0:
  16.5 120.2 all-gather.7
  143.2 110.4 all-gather.9
  260.0 110.4 all-gather.11
  376.9 110.4 all-gather.13
  493.7 110.4 all-gather.15
  610.6 110.4 all-gather.17
  727.4 110.4 all-gather.19
where the time goes:
time: 862 us; the launch traced here: 853 us
  waiting for transfers between devices  769 us (89%)
  matrix products  48.9 us (6%)
  between operations  14.1 us (2%)
  local copies, waits for them, and re-layouts  12.2 us (1%)
    all_gather x3, waiting for transfers between devices, own_step(): lax.all_gather(image_now, 'panel', axis=0, tiled=True)  340 us
    all_gather x2, waiting for transfers between devices, local(): lax.all_gather(rows_panel, 'panel', axis=0, tiled=True)  221 us
    all_gather x1, waiting for transfers between devices, local(): gathered_piece = lax.all_gather(rows_panel, 'panel', axis=0, tiled=True)  111 us
    all_gather x1, waiting for transfers between devices, local(): lax.all_gather(image_final, 'panel', axis=0, tiled=True)  97.6 us
  transfers between devices with their start and end apart: 9, of which 7 were waited for; matrix products, arithmetic and copies ran while one was open for 2% of the time, Pallas kernels for 0%

commit v1 on v0

--- a/solution.py
+++ b/solution.py
@@ -43,7 +43,19 @@
         return slice_product(own_shared, gathered_piece)
 
     def own_step(image_now):
-        return own_rows + through_own(lax.all_gather(image_now, "panel", axis=0, tiled=True))
+
+        def views_keep_up(vals):
+            return jnp.concatenate(
+                lax.all_to_all(
+                    jnp.stack(lax.axis_size("panel") * [vals], axis=0),
+                    axis_name="panel",
+                    split_axis=0,
+                    concat_axis=0,
+                ),
+                axis=0,
+            )
+
+        return own_rows + through_own(views_keep_up(image_now))
 
     image_panel = complex_product(other_form, start_rows)
     rows_panel = own_step(image_panel)

time: 862 us -> 855 us (level)
  waiting for transfers between devices: 769 us -> 520 us
  blocking collectives: 0 us -> 219 us
  starting transfers between devices: 4.47 us -> 26.4 us
  local copies, waits for them, and re-layouts: 12.2 us -> 23.9 us
    all_gather x3 -> x0, waiting for transfers between devices: 340 us -> none  [own_step(): lax.all_gather(image_now, 'panel', axis=0, tiled=True)]
    all_to_all x0 -> x2, blocking collectives: none -> 219 us  [views_keep_up(): lax.all_to_all(jnp.stack(lax.axis_size('panel') * [vals], axis=0), axis_n...]
    all_to_all x0 -> x1, waiting for transfers between devices: none -> 96 us  [views_keep_up(): lax.all_to_all(jnp.stack(lax.axis_size('panel') * [vals], axis=0), axis_n...]
    all_to_all x0 -> x1, starting transfers between devices: none -> 21.6 us  [views_keep_up(): lax.all_to_all(jnp.stack(lax.axis_size('panel') * [vals], axis=0), axis_n...]
  transfers between devices with their start and end apart: 9 -> 7, of which waited for: 7 -> 5; matrix products, arithmetic and copies ran while one was open for 2% -> 2% of each run, Pallas kernels for 0% -> 0%
where the time goes in v1:
time: 855 us; the launch traced here: 847 us
  waiting for transfers between devices  520 us (61%)
  blocking collectives  219 us (26%)
  matrix products  41 us (5%)
  starting transfers between devices  26.4 us (3%)
  local copies, waits for them, and re-layouts  23.9 us (3%)
  between operations  13.8 us (2%)
    all_to_all x2, blocking collectives, views_keep_up(): lax.all_to_all(jnp.stack(lax.axis_size('panel') * [vals], axis=0), axis_n...  219 us
    all_gather x2, waiting for transfers between devices, local(): lax.all_gather(rows_panel, 'panel', axis=0, tiled=True)  218 us
    all_gather x1, waiting for transfers between devices, local(): gathered_piece = lax.all_gather(rows_panel, 'panel', axis=0, tiled=True)  108 us
    all_gather x1, waiting for transfers between devices, local(): lax.all_gather(image_final, 'panel', axis=0, tiled=True)  97.6 us
    all_to_all x1, waiting for transfers between devices, views_keep_up(): lax.all_to_all(jnp.stack(lax.axis_size('panel') * [vals], axis=0), axis_n...  96 us
    all_to_all x1, starting transfers between devices, views_keep_up(): lax.all_to_all(jnp.stack(lax.axis_size('panel') * [vals], axis=0), axis_n...  21.6 us
  transfers between devices with their start and end apart: 7, of which 5 were waited for; matrix products, arithmetic and copies ran while one was open for 2% of the time, Pallas kernels for 0%

profile of v1, /device:TPU:4, one launch (start us, length us, event | category | flops | bytes accessed | tf_op | source)
XLA Modules:
  0.0 847.0 jit_solution(15212891502444263396)
XLA Ops:
  6.5 1.9 collective-permute-start
  8.5 4.0 fusion.111
  15.8 2.3 stack.65
  18.1 21.6 %all-to-all-start = ((f32[64,32,2,128]{3,2,1,0:T(2,128)}), f32[64,32,2,128]{3,2,1,0:T(2,128)}, u32[]{:S(2)}, u32[]{:S(2)}) async-start(f32[64,32,2,128]{3,2,1,0:T(2,128)} %stack.65), calls=%async_computation | async-start | bytes 4194304 | tf_op jit(solution)/shard_map/all_to_all | solution.py:49
  40.9 96.0 %all-to-all-done = f32[64,32,2,128]{3,2,1,0:T(2,128)} async-done(((f32[64,32,2,128]{3,2,1,0:T(2,128)}), f32[64,32,2,128]{3,2,1,0:T(2,128)}, u32[]{:S(2)}, u32[]{:S(2)}) %all-to-all-start) | async-done | bytes 2097184 | tf_op jit(solution)/shard_map/all_to_all | solution.py:49
  136.9 4.0 fusion.110
  145.1 110.1 %all-gather.5.cloned.1.call-done = f32[2048,2,128]{2,0,1:T(8,128)} async-done(((f32[32,2,128]{2,0,1:T(8,128)}), f32[2048,2,128]{2,0,1:T(8,128)}) %all-gather.5.cloned.1.call-update) | async-done | bytes 2097168 | tf_op jit(solution)/shard_map/all_gather | solution.py:64
  255.2 2.1 fusion.18
  257.3 2.0 fusion.19
  260.9 1.0 stack.72
  261.9 109.5 %all_to_all.15 = f32[64,32,2,128]{3,2,1,0:T(2,128)S(1)} all-to-all(f32[64,32,2,128]{3,2,1,0:T(2,128)S(1)} %stack.72), channel_id=1, replica_groups=mesh['box'=8,'panel'=64] {'panel'}, dimensions={0} | all-to-all | bytes 4194304 | tf_op jit(solution)/shard_map/all_to_all | solution.py:49
  371.3 1.6 fusion.109
  376.9 108.2 %all-gather.7.cloned.1.call-done = f32[2048,2,128]{2,0,1:T(8,128)} async-done(((f32[32,2,128]{2,0,1:T(8,128)}), f32[2048,2,128]{2,0,1:T(8,128)}) %all-gather.7.cloned.1.call-update) | async-done | bytes 2097168 | tf_op jit(solution)/shard_map/all_gather | solution.py:64
  485.1 2.1 fusion.20
  487.2 2.0 fusion.21
  491.8 109.5 %all_to_all.16 = f32[64,32,2,128]{3,2,1,0:T(2,128)S(1)} all-to-all(f32[64,32,2,128]{3,2,1,0:T(2,128)S(1)} %stack.79), channel_id=1, replica_groups=mesh['box'=8,'panel'=64] {'panel'}, dimensions={0} | all-to-all | bytes 4194304 | tf_op jit(solution)/shard_map/all_to_all | solution.py:49
  601.3 1.6 fusion.108
  606.6 108.4 %all-gather.9.cloned.1.call-done = f32[2048,2,128]{2,0,1:T(8,128)} async-done(((f32[32,2,128]{2,0,1:T(8,128)}), f32[2048,2,128]{2,0,1:T(8,128)}) %all-gather.9.cloned.1.call-update) | async-done | bytes 2097168 | tf_op jit(solution)/shard_map/all_gather | solution.py:67
  715.0 2.1 fusion.25
  717.1 2.0 fusion.27
  721.2 2.1 collective-permute-start.1
  723.4 4.5 fusion.112
  727.9 1.2 fusion.113
  729.1 1.3 fusion.24
  730.3 1.3 fusion
  731.6 1.3 fusion.26
  732.9 1.3 fusion.1
  734.2 97.6 %all-gather.11.cloned.1.call-done = f32[2048,2,128]{2,0,1:T(8,128)} async-done(((f32[32,2,128]{2,0,1:T(8,128)}), f32[2048,2,128]{2,0,1:T(8,128)}) %all-gather.11.cloned.1.call-update) | async-done | bytes 2097168 | tf_op jit(solution)/shard_map/all_gather | solution.py:71
  831.8 2.6 fusion.23
  834.4 2.4 fusion.22
  836.8 1.2 fusion.2
  838.0 1.2 fusion.3
  (64 shorter events, 23.3 us)
Async XLA Ops:
  6.5 6.0 collective-permute-start
  18.1 22.4 %copy-start.5 = (f32[1,32,2,2048]{3,2,1,0:T(2,128)S(1)}, f32[1,32,2,2048]{3,2,1,0:T(2,128)}, u32[]{:S(2)}) copy-start(f32[1,32,2,2048]{3,2,1,0:T(2,128)} %param.6) | copy-start | bytes 1572868
  18.1 118.8 %all-to-all-start = ((f32[64,32,2,128]{3,2,1,0:T(2,128)}), f32[64,32,2,128]{3,2,1,0:T(2,128)}, u32[]{:S(2)}, u32[]{:S(2)}) async-start(f32[64,32,2,128]{3,2,1,0:T(2,128)} %stack.65), calls=%async_computation | async-start | bytes 4194304 | tf_op jit(solution)/shard_map/all_to_all | solution.py:49
  39.7 215.5 %all-gather.5.cloned.1.call-start = ((), (), s32[]{:S(2)}) async-start(), calls=%async_computation.3 | async-start | bytes 2129920 | tf_op jit(solution)/shard_map/all_gather | solution.py:64
  144.6 340.5 %all-gather.7.cloned.1.call-start = ((), (), s32[]{:S(2)}) async-start(), calls=%async_computation.4 | async-start | bytes 2129920 | tf_op jit(solution)/shard_map/all_gather | solution.py:64
  255.2 4.1 copy-start.2
  376.7 338.3 %all-gather.9.cloned.1.call-start = ((), (), s32[]{:S(2)}) async-start(), calls=%async_computation.5 | async-start | bytes 2129920 | tf_op jit(solution)/shard_map/all_gather | solution.py:67
  485.1 4.1 copy-start.3
  606.6 225.2 %all-gather.11.cloned.1.call-start = ((), (), s32[]{:S(2)}) async-start(), calls=%async_computation.6 | async-start | bytes 2129920 | tf_op jit(solution)/shard_map/all_gather | solution.py:71
  715.0 4.1 copy-start
  721.2 6.6 collective-permute-start.1
  734.1 102.7 %copy-start.4 = (f32[96,1,2048]{2,1,0:T(1,128)S(1)}, f32[96,1,2048]{2,1,0:T(1,128)}, u32[]{:S(2)}) copy-start(f32[96,1,2048]{2,1,0:T(1,128)} %get-tuple-element.13) | copy-start | bytes 2359300
  831.8 5.0 copy-start.1
  836.8 2.4 copy-start.6
Sparse Core Ops, SparseCore 0:
  144.7 110.4 all-gather.4
  376.8 108.2 all-gather.6
  606.7 108.2 all-gather.8
  721.4 110.4 all-gather.10
